TPU v7x, 32 devices: a whole 2x2x4 slice. The times are simulated.
32 devices in a mesh: groups: 2 (over y), col: 8 (over z, x), row: 2 (over core).
Axes of the slice: x: 2, y: 2, z: 4, core: 2. Of those that a mesh axis runs over, the one named last changes fastest.
Arguments:
- down_proj: float32 [8, 2048, 7168], P(('groups', 'row'), 'col'), parts along dimension 0, may hold values from -8 to 8
- act_scale: float32 [8, 2048], P(('groups', 'row'), 'col'), parts along dimension 0, may hold values from 0.5 to 4
- block_order: int32 [512], P('groups'), parts along dimension 0, may hold values from 0 to 255, each once
Outputs:
- rotated: float32 [512, 28, 4, 2048], P(('groups', 'col'), None, 'row'), parts along dimension 0
There are 2 independent parts, one for each index of `groups`. A program takes and returns all parts, laid end to end along the dimension named above; each array names one. Nothing has to cross between parts.
Inputs may be any that keep to these rules, and one draw needn't show every extreme that they name: `block_order`: every block number appears exactly once.
All inputs are finite; a program needn't handle non-finite values.
Results may differ from a plain program's by a relative error of at most 0.000078.
Values sent between devices are 32-bit elements; how exact they have to be, the bound alone decides.
No kernel may reach another device: no remote copies, remote signals or barrier semaphores. Data moves between devices by JAX's collectives and lax.ppermute only.
A program may use at most 128 MiB of HBM per device.

v0:
```python
import jax
import jax.numpy as jnp
from jax import lax
from jax.sharding import PartitionSpec as P

BLK = 28


highest = lax.Precision.HIGHEST


def from_behind(block, axis, distance):
    devices = range(lax.axis_size(axis))
    route = [((i - distance) % len(devices), i) for i in devices]
    return lax.ppermute(block, axis, route)


def joint_rotation(gram_matrix):
    square = jnp.einsum("pij,pjk->pik", gram_matrix, gram_matrix, precision=highest)
    lower_factor = jnp.linalg.cholesky(square)
    solved = lax.linalg.triangular_solve(lower_factor, gram_matrix, left_side=True, lower=True)
    return jnp.swapaxes(solved, 1, 2)


def pair_gram(panels):
    return jnp.einsum("pkr,plr->pkl", panels, panels, precision=highest)


def rotate_pairs(rotation, panels):
    return jnp.einsum("pkl,pkr->plr", rotation, panels, precision=highest)


def local_panels(piece):
    panels = piece.reshape(piece.shape[1], piece.shape[2], -1)
    return (panels, pair_gram(panels))


def outgoing_panels(blocks, picked, col_count, extent):
    experts_here, hidden_here = (blocks.shape[0], blocks.shape[1])
    ordered = jnp.take(blocks, picked, axis=2)
    ordered = ordered.reshape(experts_here, hidden_here, col_count, extent // 2, 2 * BLK)
    ordered = jnp.transpose(ordered, (2, 3, 4, 0, 1))
    return ordered.reshape(col_count, extent // 2, 2 * BLK, experts_here, 1, hidden_here)


def shards(down_proj, act_scale, block_order):
    col_count = lax.axis_size("col")
    experts_here, hidden_here, width = down_proj.shape
    block_count = width // BLK
    per_device = block_count // col_count
    scaled = down_proj * act_scale[:, :, None]
    blocks = scaled.reshape(experts_here, hidden_here, block_count, BLK)
    sending = outgoing_panels(blocks, block_order, col_count, per_device)
    panels, partial_sums = local_panels(
        lax.all_to_all(sending, "col", split_axis=0, concat_axis=4, tiled=True)
    )
    gram_all = lax.psum(partial_sums, "row")
    rotation = joint_rotation(gram_all)
    first_pass = rotate_pairs(rotation, panels)
    leading = first_pass[:, :BLK]
    trailing = first_pass[:, BLK:]
    carried = from_behind(leading[-1:], "col", 1)
    moved = jnp.concatenate([carried, leading[:-1]], axis=0)
    next_panels = jnp.concatenate([moved, trailing], axis=1)
    next_total = lax.psum(pair_gram(next_panels), "row")
    second_pass = rotate_pairs(joint_rotation(next_total), next_panels)
    return second_pass.reshape(per_device, BLK, experts_here, -1)


def solution(mesh):
    return jax.shard_map(
        shards,
        mesh=mesh,
        in_specs=(P(("groups", "row"), "col", None), P(("groups", "row"), "col"), P("groups")),
        out_specs=P(("groups", "col"), None, "row", None),
        check_vma=False,
    )
```

profile of v0, /device:TPU:0, one launch (start us, length us, event | category | flops | bytes accessed | tf_op | source)
XLA Modules:
  0.0 913.6 jit_solution(10657160507606696045)
XLA Ops:
  8.4 13.5 %broadcast_multiply_fusion = f32[2,256,7168]{2,1,0:T(8,128)} fusion(f32[2,256,7168]{2,1,0:T(8,128)} %param.6, f32[2,256]{1,0:T(2,128)} %param.7), kind=kLoop, calls=%fused_computation.5 | loop fusion | flops 3670016 | bytes 29362176 | tf_op jit(solution)/shard_map/mul | solution.py:51
  21.9 22.0 %copy.17 = f32[2,256,7168]{1,0,2:T(2,128)} copy(f32[2,256,7168]{2,1,0:T(8,128)} %broadcast_multiply_fusion) | data formatting | bytes 29360128 | tf_op jit(solution)/shard_map/mul | solution.py:51
  43.9 30.5 %gather_fusion = f32[256,2,256,28]{2,1,3,0:T(2,128)} fusion(f32[2,256,256,28]{1,0,3,2:T(2,128)} %bitcast.47, s32[1024]{0:T(1024)S(1)} %pad_clamp_fusion), kind=kCustom, calls=%fused_computation | custom fusion | bytes 29361152 | tf_op jit(solution)/shard_map/jit(_take)/gather | solution.py:40
  74.5 11.7 %select_bitcast_fusion = f32[8,16,56,2,1,256]{5,3,2,1,4,0:T(2,128)S(1)} fusion(f32[2,256,8,16,56]{1,0,4,3,2:T(2,128)} %bitcast.46, pred[8,16,56]{2,1,0:T(8,128)(4,1)S(1)} %broadcast_in_dim.25), kind=kLoop, calls=%fused_computation.2 | loop fusion | flops 3670016 | bytes 29367296 | tf_op jit(solution)/shard_map/reshape | solution.py:43
  86.2 325.3 %all_to_all.15 = f32[8,16,56,2,1,256]{5,3,2,1,4,0:T(2,128)} all-to-all(f32[8,16,56,2,1,256]{5,3,2,1,4,0:T(2,128)S(1)} %select_bitcast_fusion), channel_id=1, replica_groups=mesh['groups'=2,'col'=8,'row'=2] {'col'}, dimensions={0} | all-to-all | bytes 29360128 | tf_op jit(solution)/shard_map/all_to_all | solution.py:55
  411.5 22.0 %copy.19 = f32[1,16,56,2,8,1,256]{6,4,3,2,1,5,0:T(8,128)} copy(f32[1,16,56,2,8,1,256]{6,3,2,1,4,5,0:T(2,128)} %bitcast.48) | data formatting | bytes 29360128 | tf_op jit(solution)/shard_map/all_to_all | solution.py:55
  433.4 16.4 %reshape.39 = f32[16,56,4096]{2,1,0:T(8,128)} reshape(f32[1,16,56,2,8,1,256]{6,4,3,2,1,5,0:T(8,128)} %copy.19) | data formatting | bytes 29360128 | tf_op jit(solution)/shard_map/reshape | solution.py:34
  449.8 17.7 %fusion.10 = f32[16,56,56]{2,1,0:T(8,128)} fusion(f32[16,56,4096]{2,1,0:T(8,128)} %reshape.39), kind=kOutput, calls=%fused_computation.27 | convolution fusion | flops 2466250752 | bytes 14880768 | tf_op jit(solution)/shard_map/pkr,plr->pkl/dot_general | solution.py:26
  467.7 17.6 %all-reduce.3.cloned.1.call-done = f32[16,56,56]{2,1,0:T(8,128)} async-done(((f32[16,56,56]{2,1,0:T(8,128)}), f32[16,56,56]{2,1,0:T(8,128)}) %all-reduce.3.cloned.1.call-update) | async-done | bytes 200720 | tf_op jit(solution)/shard_map/psum | solution.py:57
  485.3 2.0 fusion.11
  487.6 82.2 %custom-call.8 = f32[16,56,56]{2,1,0:T(8,128)S(1)} custom-call(f32[16,56,56]{2,1,0:T(8,128)S(1)} %fusion.7), custom_call_target="Cholesky" | custom-call | tf_op jit(solution)/shard_map/jit(cholesky)/cholesky | solution.py:20
  570.1 68.9 %custom-call.9 = f32[16,1,56,56]{2,3,1,0:T(8,128)S(1)} custom-call(f32[16,1,56,56]{3,2,1,0:T(8,128)S(1)} %select_bitcast_fusion.2), custom_call_target="InvertDiagBlocksLowerTriangular" | custom-call | tf_op jit(solution)/shard_map/triangular_solve/custom-call.0 | solution.py:21
  638.9 2.0 fusion.5
  640.9 17.3 %fusion.12 = f32[16,56,4096]{2,1,0:T(8,128)S(1)} fusion(f32[16,56,56]{2,1,0:T(8,128)S(1)} %fusion.5, f32[16,56,4096]{2,1,0:T(8,128)} %reshape.39), kind=kOutput, calls=%fused_computation.29 | convolution fusion | flops 2466250752 | bytes 29560832 | tf_op jit(solution)/shard_map/pkl,pkr->plr/dot_general | solution.py:30
  660.1 3.6 slice.24
  663.7 4.5 slice.25
  668.2 7.0 collective-permute-done
  675.2 19.9 %fusion.1 = f32[16,56,56]{2,1,0:T(8,128)} fusion(f32[16,28,4096]{2,1,0:T(8,128)} %slice.25, f32[15,28,4096]{2,1,0:T(8,128)} %slice.24, f32[1,28,4096]{2,1,0:T(8,128)S(1)} %collective-permute-done), kind=kOutput, calls=%fused_computation.4 | convolution fusion | flops 2473590784 | bytes 14880768 | tf_op jit(solution)/shard_map/pkr,plr->pkl/dot_general | solution.py:26
  695.1 17.1 %all-reduce.5.cloned.1.call-done = f32[16,56,56]{2,1,0:T(8,128)} async-done(((f32[16,56,56]{2,1,0:T(8,128)}), f32[16,56,56]{2,1,0:T(8,128)}) %all-reduce.5.cloned.1.call-update) | async-done | bytes 200720 | tf_op jit(solution)/shard_map/psum | solution.py:65
  712.2 2.0 fusion.13
  714.4 82.2 %custom-call.10 = f32[16,56,56]{2,1,0:T(8,128)S(1)} custom-call(f32[16,56,56]{2,1,0:T(8,128)S(1)} %fusion.4), custom_call_target="Cholesky" | custom-call | tf_op jit(solution)/shard_map/jit(cholesky)/cholesky | solution.py:20
  796.9 68.9 %custom-call.11 = f32[16,1,56,56]{2,3,1,0:T(8,128)S(1)} custom-call(f32[16,1,56,56]{3,2,1,0:T(8,128)S(1)} %select_bitcast_fusion.1), custom_call_target="InvertDiagBlocksLowerTriangular" | custom-call | tf_op jit(solution)/shard_map/triangular_solve/custom-call.0 | solution.py:21
  867.8 19.3 %fusion = f32[16,56,4096]{2,1,0:T(8,128)} fusion(f32[16,56,56]{2,1,0:T(8,128)S(1)} %fusion.2, f32[16,28,4096]{2,1,0:T(8,128)} %slice.25, f32[15,28,4096]{2,1,0:T(8,128)} %slice.24, f32[1,28,4096]{2,1,0:T(8,128)S(1)} %collective-permute-done), kind=kOutput, calls=%fused_computation.3 | convolution fusion | flops 2473590784 | bytes 29560832 | tf_op jit(solution)/shard_map/pkl,pkr->plr/dot_general | solution.py:30
  887.1 19.4 %reshape.40 = f32[32,28,2,2048]{3,2,1,0:T(2,128)} reshape(f32[16,56,4096]{2,1,0:T(8,128)} %fusion) | data formatting | bytes 29360128 | tf_op jit(solution)/shard_map/reshape | solution.py:67
  (25 shorter events, 6.8 us)
Async XLA Ops:
  6.5 478.8 %all-reduce.3.cloned.1.call-start = ((), (), s32[]{:S(2)}) async-start(), calls=%async_computation.1 | async-start | bytes 917504 | tf_op jit(solution)/shard_map/psum | solution.py:57
  467.6 244.6 %all-reduce.5.cloned.1.call-start = ((), (), s32[]{:S(2)}) async-start(), calls=%async_computation.2 | async-start | bytes 917504 | tf_op jit(solution)/shard_map/psum | solution.py:65
  658.2 16.9 %collective-permute-start = (f32[1,28,4096]{2,1,0:T(8,128)S(1)}, f32[1,28,4096]{2,1,0:T(8,128)S(1)}, u32[]{:S(2)}, u32[]{:S(2)}) collective-permute-start(f32[1,28,4096]{2,1,0:T(8,128)S(1)} %slice.23), channel_id=1, source_target_pairs={{14,0},{0,2},{2,4},{4,6},{6,8},{8,10},{10,12},{12,14},{15,1},{1,3}... | collective-permute-start | bytes 1376264 | tf_op jit(solution)/shard_map/ppermute | solution.py:15
Sparse Core Ops, SparseCore 0:
  467.7 17.5 all-reduce.2
  695.2 16.9 all-reduce.4
where the time goes:
time: 921 us; the launch traced here: 914 us
  other arithmetic  329 us (36%)
  blocking collectives  325 us (35%)
  local copies, waits for them, and re-layouts  119 us (13%)
  matrix products  82.1 us (9%)
  waiting for transfers between devices  41.7 us (5%)
  between operations  13.8 us (1%)
    all_to_all x1, blocking collectives, shards(): lax.all_to_all(sending, 'col', split_axis=0, concat_axis=4, tiled=True)  325 us
    another operation x7, other arithmetic, joint_rotation(): lower_factor = jnp.linalg.cholesky(square)  165 us
    another operation x5, other arithmetic, joint_rotation(): lax.linalg.triangular_solve(lower_factor, gram_matrix, left_side=True, lo...  138 us
    dot_general x2, matrix products, pair_gram(): return jnp.einsum('pkr,plr->pkl', panels, panels, precision=highest)  37.6 us
    dot_general x2, matrix products, rotate_pairs(): return jnp.einsum('pkl,pkr->plr', rotation, panels, precision=highest)  36.5 us
    gather x1, local copies, waits for them, and re-layouts, outgoing_panels(): ordered = jnp.take(blocks, picked, axis=2)  30.5 us
    mul x1, local copies, waits for them, and re-layouts, shards(): scaled = down_proj * act_scale[:, :, None]  22 us
    all_to_all x1, local copies, waits for them, and re-layouts, shards(): lax.all_to_all(sending, 'col', split_axis=0, concat_axis=4, tiled=True)  22 us
  transfers between devices with their start and end apart: 3, of which 3 were waited for; matrix products, arithmetic and copies ran while one was open for 1% of the time, Pallas kernels for 0%

commit v1 on v0

--- a/solution.py
+++ b/solution.py
@@ -1,6 +1,8 @@
 import jax
 import jax.numpy as jnp
 from jax import lax
+from jax.experimental import pallas as pl
+from jax.experimental.pallas import tpu as pltpu
 from jax.sharding import PartitionSpec as P
 
 BLK = 28
@@ -15,19 +17,49 @@
     return lax.ppermute(block, axis, route)
 
 
-def joint_rotation(gram_matrix):
+def chol_solve_kernel(sq_ref, s_ref, x_ref, a_ref):
+    n = sq_ref.shape[1]
+    a_ref[...] = sq_ref[...]
+    x_ref[...] = s_ref[...]
+    for k in range(n):
+        r0 = (k // 8) * 8
+        rows = n - r0
+        i_idx = lax.broadcasted_iota(jnp.int32, (1, rows, 1), 1) + r0
+        j_idx = lax.broadcasted_iota(jnp.int32, (1, 1, n), 2)
+        a_part = a_ref[:, r0:, :]
+        d = jnp.sqrt(a_ref[:, k:k + 1, k:k + 1])
+        lcol = jnp.where(i_idx >= k, a_part[:, :, k:k + 1] / d, 0.0)
+        lrow = jnp.where(j_idx >= k, a_ref[:, k:k + 1, :] / d, 0.0)
+        a_ref[:, r0:, :] = a_part - lcol * lrow
+        xk = x_ref[:, k:k + 1, :] / d
+        b_part = x_ref[:, r0:, :]
+        b_part = b_part - jnp.where(i_idx > k, lcol, 0.0) * xk
+        x_ref[:, r0:, :] = jnp.where(i_idx == k, xk, b_part)
+
+
+def chol_solve(square, gram_matrix):
+    batch, n, _ = gram_matrix.shape
+    spec = pl.BlockSpec((batch, n, n), lambda: (0, 0, 0))
+    return pl.pallas_call(
+        chol_solve_kernel,
+        out_shape=jax.ShapeDtypeStruct(gram_matrix.shape, jnp.float32),
+        in_specs=[spec, spec],
+        out_specs=spec,
+        scratch_shapes=[pltpu.VMEM((batch, n, n), jnp.float32)],
+    )(square, gram_matrix)
+
+
+def solved_rotation(gram_matrix):
     square = jnp.einsum("pij,pjk->pik", gram_matrix, gram_matrix, precision=highest)
-    lower_factor = jnp.linalg.cholesky(square)
-    solved = lax.linalg.triangular_solve(lower_factor, gram_matrix, left_side=True, lower=True)
-    return jnp.swapaxes(solved, 1, 2)
+    return chol_solve(square, gram_matrix)
 
 
 def pair_gram(panels):
     return jnp.einsum("pkr,plr->pkl", panels, panels, precision=highest)
 
 
-def rotate_pairs(rotation, panels):
-    return jnp.einsum("pkl,pkr->plr", rotation, panels, precision=highest)
+def rotate_pairs(solved, panels):
+    return jnp.einsum("plk,pkr->plr", solved, panels, precision=highest)
 
 
 def local_panels(piece):
@@ -55,15 +87,14 @@
         lax.all_to_all(sending, "col", split_axis=0, concat_axis=4, tiled=True)
     )
     gram_all = lax.psum(partial_sums, "row")
-    rotation = joint_rotation(gram_all)
-    first_pass = rotate_pairs(rotation, panels)
+    first_pass = rotate_pairs(solved_rotation(gram_all), panels)
     leading = first_pass[:, :BLK]
     trailing = first_pass[:, BLK:]
     carried = from_behind(leading[-1:], "col", 1)
     moved = jnp.concatenate([carried, leading[:-1]], axis=0)
     next_panels = jnp.concatenate([moved, trailing], axis=1)
     next_total = lax.psum(pair_gram(next_panels), "row")
-    second_pass = rotate_pairs(joint_rotation(next_total), next_panels)
+    second_pass = rotate_pairs(solved_rotation(next_total), next_panels)
     return second_pass.reshape(per_device, BLK, experts_here, -1)
 
 

time: 921 us -> 639 us (0.69)
  other arithmetic: 329 us -> 26.6 us
  Pallas kernels: 0 us -> 23.1 us
    another operation x12 -> x0, other arithmetic: 303 us -> none  [the longest x7 165 us: joint_rotation(): lower_factor = jnp.linalg.cholesky(square)]
    pallas_call x0 -> x2, Pallas kernels: none -> 23.1 us  [chol_solve(): pl.pallas_call(chol_solve_kernel, out_shape=jax.ShapeDtypeStruct(gram_mat...]
where the time goes in v1:
time: 639 us; the launch traced here: 632 us
  blocking collectives  325 us (51%)
  local copies, waits for them, and re-layouts  119 us (19%)
  matrix products  80.2 us (13%)
  waiting for transfers between devices  41.7 us (7%)
  other arithmetic  26.6 us (4%)
  Pallas kernels  23.1 us (4%)
  between operations  13.9 us (2%)
    all_to_all x1, blocking collectives, shards(): lax.all_to_all(sending, 'col', split_axis=0, concat_axis=4, tiled=True)  325 us
    dot_general x2, matrix products, pair_gram(): return jnp.einsum('pkr,plr->pkl', panels, panels, precision=highest)  37.6 us
    dot_general x2, matrix products, rotate_pairs(): return jnp.einsum('plk,pkr->plr', solved, panels, precision=highest)  37 us
    gather x1, local copies, waits for them, and re-layouts, outgoing_panels(): ordered = jnp.take(blocks, picked, axis=2)  30.5 us
    pallas_call x2, Pallas kernels, chol_solve(): pl.pallas_call(chol_solve_kernel, out_shape=jax.ShapeDtypeStruct(gram_mat...  23.1 us
    mul x1, local copies, waits for them, and re-layouts, shards(): scaled = down_proj * act_scale[:, :, None]  22 us
    all_to_all x1, local copies, waits for them, and re-layouts, shards(): lax.all_to_all(sending, 'col', split_axis=0, concat_axis=4, tiled=True)  22 us
    reshape x1, local copies, waits for them, and re-layouts, shards(): return second_pass.reshape(per_device, BLK, experts_here, -1)  19.4 us
  transfers between devices with their start and end apart: 3, of which 3 were waited for; matrix products, arithmetic and copies ran while one was open for 1% of the time, Pallas kernels for 0%

profile of v1, /device:TPU:0, one launch (start us, length us, event | category | flops | bytes accessed | tf_op | source)
XLA Modules:
  0.0 631.7 jit_solution(12220698139732642383)
XLA Ops:
  6.5 0.7 compare_and_fusion
  7.2 0.7 compare_select_fusion
  8.4 13.5 %broadcast_multiply_fusion = f32[2,256,7168]{2,1,0:T(8,128)} fusion(f32[2,256,7168]{2,1,0:T(8,128)} %param.3, f32[2,256]{1,0:T(2,128)} %param.4), kind=kLoop, calls=%fused_computation.5 | loop fusion | flops 3670016 | bytes 29362176 | tf_op jit(solution)/shard_map/mul | solution.py:83
  21.9 22.0 %copy.6 = f32[2,256,7168]{1,0,2:T(2,128)} copy(f32[2,256,7168]{2,1,0:T(8,128)} %broadcast_multiply_fusion) | data formatting | bytes 29360128 | tf_op jit(solution)/shard_map/mul | solution.py:83
  43.9 30.5 %gather_fusion = f32[256,2,256,28]{2,1,3,0:T(2,128)} fusion(f32[2,256,256,28]{1,0,3,2:T(2,128)} %bitcast.27, s32[1024]{0:T(1024)S(1)} %pad_clamp_fusion), kind=kCustom, calls=%fused_computation | custom fusion | bytes 29361152 | tf_op jit(solution)/shard_map/jit(_take)/gather | solution.py:72
  74.5 11.7 %select_bitcast_fusion = f32[8,16,56,2,1,256]{5,3,2,1,4,0:T(2,128)S(1)} fusion(f32[2,256,8,16,56]{1,0,4,3,2:T(2,128)} %bitcast.26, pred[8,16,56]{2,1,0:T(8,128)(4,1)S(1)} %broadcast_in_dim.21), kind=kLoop, calls=%fused_computation.2 | loop fusion | flops 3670016 | bytes 29367296 | tf_op jit(solution)/shard_map/reshape | solution.py:75
  86.2 325.3 %all_to_all.15 = f32[8,16,56,2,1,256]{5,3,2,1,4,0:T(2,128)} all-to-all(f32[8,16,56,2,1,256]{5,3,2,1,4,0:T(2,128)S(1)} %select_bitcast_fusion), channel_id=1, replica_groups=mesh['groups'=2,'col'=8,'row'=2] {'col'}, dimensions={0} | all-to-all | bytes 29360128 | tf_op jit(solution)/shard_map/all_to_all | solution.py:87
  411.5 22.0 %copy.8 = f32[1,16,56,2,8,1,256]{6,4,3,2,1,5,0:T(8,128)} copy(f32[1,16,56,2,8,1,256]{6,3,2,1,4,5,0:T(2,128)} %bitcast.28) | data formatting | bytes 29360128 | tf_op jit(solution)/shard_map/all_to_all | solution.py:87
  433.4 16.5 %reshape.27 = f32[16,56,4096]{2,1,0:T(8,128)} reshape(f32[1,16,56,2,8,1,256]{6,4,3,2,1,5,0:T(8,128)} %copy.8) | data formatting | bytes 29360128 | tf_op jit(solution)/shard_map/reshape | solution.py:66
  449.9 17.7 %fusion.4 = f32[16,56,56]{2,1,0:T(8,128)} fusion(f32[16,56,4096]{2,1,0:T(8,128)} %reshape.27), kind=kOutput, calls=%fused_computation.11 | convolution fusion | flops 2466250752 | bytes 14880768 | tf_op jit(solution)/shard_map/pkr,plr->pkl/dot_general | solution.py:58
  467.7 17.7 %all-reduce.3.cloned.1.call-done.s_ref = f32[16,56,56]{2,1,0:T(8,128)} async-done(((f32[16,56,56]{2,1,0:T(8,128)}), f32[16,56,56]{2,1,0:T(8,128)}) %all-reduce.3.cloned.1.call-update) | async-done | bytes 200720 | tf_op jit(solution)/shard_map/psum | solution.py:89
  485.3 2.8 fusion.5.sq_ref
  488.1 11.5 %shard_map.37 = f32[16,56,56]{2,1,0:T(8,128)} custom-call(f32[16,56,56]{2,1,0:T(8,128)} %fusion.5.sq_ref, f32[16,56,56]{2,1,0:T(8,128)} %all-reduce.3.cloned.1.call-done.s_ref), custom_call_target="tpu_custom_call" | custom-call | tf_op jit(solution)/shard_map/pallas_call | solution.py:43
  499.7 17.5 %fusion.6 = f32[16,56,4096]{2,1,0:T(8,128)S(1)} fusion(f32[16,56,56]{2,1,0:T(8,128)} %shard_map.37, f32[16,56,4096]{2,1,0:T(8,128)} %reshape.27), kind=kOutput, calls=%fused_computation.13 | convolution fusion | flops 2466250752 | bytes 29560832 | tf_op jit(solution)/shard_map/plk,pkr->plr/dot_general | solution.py:62
  517.3 1.8 collective-permute-start
  519.1 3.6 slice.18
  522.7 4.5 slice.19
  527.2 7.0 %collective-permute-done = f32[1,28,4096]{2,1,0:T(8,128)S(1)} collective-permute-done((f32[1,28,4096]{2,1,0:T(8,128)S(1)}, f32[1,28,4096]{2,1,0:T(8,128)S(1)}, u32[]{:S(2)}, u32[]{:S(2)}) %collective-permute-start) | collective-permute-done | bytes 458784 | tf_op jit(solution)/shard_map/ppermute | solution.py:17
  534.2 19.9 %fusion.1 = f32[16,56,56]{2,1,0:T(8,128)} fusion(f32[16,28,4096]{2,1,0:T(8,128)} %slice.19, f32[15,28,4096]{2,1,0:T(8,128)} %slice.18, f32[1,28,4096]{2,1,0:T(8,128)S(1)} %collective-permute-done), kind=kOutput, calls=%fused_computation.4 | convolution fusion | flops 2473590784 | bytes 14880768 | tf_op jit(solution)/shard_map/pkr,plr->pkl/dot_general | solution.py:58
  554.1 17.1 %all-reduce.5.cloned.1.call-done.s_ref = f32[16,56,56]{2,1,0:T(8,128)} async-done(((f32[16,56,56]{2,1,0:T(8,128)}), f32[16,56,56]{2,1,0:T(8,128)}) %all-reduce.5.cloned.1.call-update) | async-done | bytes 200720 | tf_op jit(solution)/shard_map/psum | solution.py:96
  571.2 2.8 fusion.7.sq_ref
  574.0 11.5 %shard_map.38 = f32[16,56,56]{2,1,0:T(8,128)} custom-call(f32[16,56,56]{2,1,0:T(8,128)} %fusion.7.sq_ref, f32[16,56,56]{2,1,0:T(8,128)} %all-reduce.5.cloned.1.call-done.s_ref), custom_call_target="tpu_custom_call" | custom-call | tf_op jit(solution)/shard_map/pallas_call | solution.py:43
  585.5 19.5 %fusion = f32[16,56,4096]{2,1,0:T(8,128)} fusion(f32[16,56,56]{2,1,0:T(8,128)} %shard_map.38, f32[16,28,4096]{2,1,0:T(8,128)} %slice.19, f32[15,28,4096]{2,1,0:T(8,128)} %slice.18, f32[1,28,4096]{2,1,0:T(8,128)S(1)} %collective-permute-done), kind=kOutput, calls=%fused_computation.3 | convolution fusion | flops 2473590784 | bytes 29560832 | tf_op jit(solution)/shard_map/plk,pkr->plr/dot_general | solution.py:62
  605.0 19.4 %reshape.28 = f32[32,28,2,2048]{3,2,1,0:T(2,128)} reshape(f32[16,56,4096]{2,1,0:T(8,128)} %fusion) | data formatting | bytes 29360128 | tf_op jit(solution)/shard_map/reshape | solution.py:98
  (9 shorter events, 0.6 us)
Async XLA Ops:
  6.5 478.8 %all-reduce.3.cloned.1.call-start = ((), (), s32[]{:S(2)}) async-start(), calls=%async_computation.1 | async-start | bytes 917504 | tf_op jit(solution)/shard_map/psum | solution.py:89
  467.6 103.6 %all-reduce.5.cloned.1.call-start = ((), (), s32[]{:S(2)}) async-start(), calls=%async_computation.2 | async-start | bytes 917504 | tf_op jit(solution)/shard_map/psum | solution.py:96
  517.3 16.9 %collective-permute-start = (f32[1,28,4096]{2,1,0:T(8,128)S(1)}, f32[1,28,4096]{2,1,0:T(8,128)S(1)}, u32[]{:S(2)}, u32[]{:S(2)}) collective-permute-start(f32[1,28,4096]{2,1,0:T(8,128)S(1)} %slice.17), channel_id=1, source_target_pairs={{14,0},{0,2},{2,4},{4,6},{6,8},{8,10},{10,12},{12,14},{15,1},{1,3}... | collective-permute-start | bytes 1376264 | tf_op jit(solution)/shard_map/ppermute | solution.py:17
Sparse Core Ops, SparseCore 0:
  467.7 17.5 all-reduce.2
  554.2 16.9 all-reduce.4

commit v2 on v1

v2 whole, which is shorter than its diff:
```python
import jax
import jax.numpy as jnp
from jax import lax
from jax.experimental import pallas as pl
from jax.experimental.pallas import tpu as pltpu
from jax.sharding import PartitionSpec as P

BLK = 28


highest = lax.Precision.HIGHEST


def chol_solve_kernel(sq_ref, s_ref, x_ref, a_ref):
    n = sq_ref.shape[1]
    a_ref[...] = sq_ref[...]
    x_ref[...] = s_ref[...]
    for k in range(n):
        r0 = (k // 8) * 8
        rows = n - r0
        i_idx = lax.broadcasted_iota(jnp.int32, (1, rows, 1), 1) + r0
        j_idx = lax.broadcasted_iota(jnp.int32, (1, 1, n), 2)
        a_part = a_ref[:, r0:, :]
        d = jnp.sqrt(a_ref[:, k:k + 1, k:k + 1])
        lcol = jnp.where(i_idx >= k, a_part[:, :, k:k + 1] / d, 0.0)
        lrow = jnp.where(j_idx >= k, a_ref[:, k:k + 1, :] / d, 0.0)
        a_ref[:, r0:, :] = a_part - lcol * lrow
        xk = x_ref[:, k:k + 1, :] / d
        b_part = x_ref[:, r0:, :]
        b_part = b_part - jnp.where(i_idx > k, lcol, 0.0) * xk
        x_ref[:, r0:, :] = jnp.where(i_idx == k, xk, b_part)


def chol_solve(square, gram_matrix):
    batch, n, _ = gram_matrix.shape
    spec = pl.BlockSpec((batch, n, n), lambda: (0, 0, 0))
    return pl.pallas_call(
        chol_solve_kernel,
        out_shape=jax.ShapeDtypeStruct(gram_matrix.shape, jnp.float32),
        in_specs=[spec, spec],
        out_specs=spec,
        scratch_shapes=[pltpu.VMEM((batch, n, n), jnp.float32)],
    )(square, gram_matrix)


def mm(spec, a, b):
    return jnp.einsum(spec, a, b, precision=highest)


def solved_rotation(gram_matrix):
    return chol_solve(mm("pij,pjk->pik", gram_matrix, gram_matrix), gram_matrix)


def shards(down_proj, act_scale, block_order):
    col_count = lax.axis_size("col")
    me = lax.axis_index("col")
    experts_here, hidden_here, width = down_proj.shape
    block_count = width // BLK
    per_device = block_count // col_count
    panels_here = per_device // 2
    rows_here = experts_here * hidden_here
    scaled = down_proj * act_scale[:, :, None]
    blocks = scaled.reshape(experts_here, hidden_here, block_count, BLK)
    span = jnp.arange(per_device + 2, dtype=jnp.int32)

    received = []
    for d in range(col_count):
        dest = (me + d) % col_count
        picked = jnp.take(block_order, (dest * per_device - 2 + span) % block_count)
        piece = jnp.take(blocks, picked, axis=2)
        piece = jnp.transpose(piece, (2, 3, 0, 1)).reshape(panels_here + 1, 2 * BLK, rows_here)
        if d:
            route = [(i, (i + d) % col_count) for i in range(col_count)]
            piece = lax.ppermute(piece, "col", route)
        received.append(piece)

    grams = sum(mm("pkr,plr->pkl", r, r) for r in received)
    cross = sum(mm("pkr,plr->pkl", r[:-1], r[1:]) for r in received)
    totals = lax.psum(jnp.concatenate([grams, cross], axis=0), "row")
    grams, cross = totals[: panels_here + 1], totals[panels_here + 1:]

    first = solved_rotation(grams)
    top = first[:-1, :BLK]
    bottom = first[1:, BLK:]
    g_top = mm("pik,pjk->pij", mm("pik,pkl->pil", top, grams[:-1]), top)
    g_bottom = mm("pik,pjk->pij", mm("pik,pkl->pil", bottom, grams[1:]), bottom)
    g_cross = mm("pik,pjk->pij", mm("pik,pkl->pil", top, cross), bottom)
    second_gram = jnp.concatenate(
        [
            jnp.concatenate([g_top, g_cross], axis=2),
            jnp.concatenate([jnp.swapaxes(g_cross, 1, 2), g_bottom], axis=2),
        ],
        axis=1,
    )
    second = solved_rotation(second_gram)
    lead = mm("plk,pkm->plm", second[:, :, :BLK], top)
    trail = mm("plk,pkm->plm", second[:, :, BLK:], bottom)

    out = jnp.zeros((per_device, BLK, experts_here, hidden_here * col_count), jnp.float32)
    for d, r in enumerate(received):
        src = (me - d) % col_count
        part = mm("plk,pkr->plr", lead, r[:-1]) + mm("plk,pkr->plr", trail, r[1:])
        part = part.reshape(per_device, BLK, experts_here, hidden_here)
        out = lax.dynamic_update_slice(out, part, (0, 0, 0, src * hidden_here))
    return out


def solution(mesh):
    return jax.shard_map(
        shards,
        mesh=mesh,
        in_specs=(P(("groups", "row"), "col", None), P(("groups", "row"), "col"), P("groups")),
        out_specs=P(("groups", "col"), None, "row", None),
        check_vma=False,
    )
```

time: 639 us -> 629 us (0.984)
  blocking collectives: 325 us -> 0 us
  waiting for transfers between devices: 41.7 us -> 192 us
  local copies, waits for them, and re-layouts: 119 us -> 198 us
  matrix products: 80.2 us -> 119 us
  starting transfers between devices: 1.86 us -> 31 us
  other arithmetic: 26.6 us -> 41.1 us
    all_to_all x1 -> x0, blocking collectives: 325 us -> none  [shards(): lax.all_to_all(sending, 'col', split_axis=0, concat_axis=4, tiled=True)]
    ppermute x1 -> x7, waiting for transfers between devices: 6.95 us -> 118 us  [shards(): piece = lax.ppermute(piece, 'col', route)]
    gather x1 -> x16, local copies, waits for them, and re-layouts: 30.5 us -> 80.9 us  [the longest x8 74.5 us: shards(): piece = jnp.take(blocks, picked, axis=2)]
    psum x2 -> x1, waiting for transfers between devices: 34.7 us -> 74.6 us  [shards(): totals = lax.psum(jnp.concatenate([grams, cross], axis=0), 'row')]
    dot_general x6 -> x42, matrix products: 80.2 us -> 119 us  [mm(): return jnp.einsum(spec, a, b, precision=highest)]
    ppermute x1 -> x7, starting transfers between devices: 1.82 us -> 31 us  [shards(): piece = lax.ppermute(piece, 'col', route)]
    transpose x0 -> x8, other arithmetic: none -> 26.1 us  [shards(): jnp.transpose(piece, (2, 3, 0, 1))]
    all_to_all x1 -> x0, local copies, waits for them, and re-layouts: 22 us -> none  [shards(): lax.all_to_all(sending, 'col', split_axis=0, concat_axis=4, tiled=True)]
  transfers between devices with their start and end apart: 3 -> 8, of which waited for: 3 -> 4; matrix products, arithmetic and copies ran while one was open for 1% -> 28% of each run, Pallas kernels for 0% -> 0%
where the time goes in v2:
time: 629 us; the launch traced here: 621 us
  local copies, waits for them, and re-layouts  198 us (31%)
  waiting for transfers between devices  192 us (31%)
  matrix products  119 us (19%)
  other arithmetic  41.1 us (7%)
  starting transfers between devices  31 us (5%)
  Pallas kernels  23.7 us (4%)
  between operations  15 us (2%)
    dot_general x42, matrix products, mm(): return jnp.einsum(spec, a, b, precision=highest)  119 us
    ppermute x7, waiting for transfers between devices, shards(): piece = lax.ppermute(piece, 'col', route)  118 us
    psum x1, waiting for transfers between devices, shards(): totals = lax.psum(jnp.concatenate([grams, cross], axis=0), 'row')  74.6 us
    gather x8, local copies, waits for them, and re-layouts, shards(): piece = jnp.take(blocks, picked, axis=2)  74.5 us
    ppermute x7, starting transfers between devices, shards(): piece = lax.ppermute(piece, 'col', route)  31 us
    reshape x8, local copies, waits for them, and re-layouts, shards(): jnp.transpose(piece, (2, 3, 0, 1))  30 us
    reshape x8, local copies, waits for them, and re-layouts, shards(): part = part.reshape(per_device, BLK, experts_here, hidden_here)  27.3 us
    transpose x8, other arithmetic, shards(): jnp.transpose(piece, (2, 3, 0, 1))  26.1 us
  transfers between devices with their start and end apart: 8, of which 4 were waited for; matrix products, arithmetic and copies ran while one was open for 28% of the time, Pallas kernels for 0%

profile of v2, /device:TPU:0, one launch (start us, length us, event | category | flops | bytes accessed | tf_op | source)
XLA Modules:
  0.0 620.9 jit_solution(14325069548961039224)
XLA Ops:
  8.0 13.5 %broadcast_multiply_fusion = f32[2,256,7168]{2,1,0:T(8,128)} fusion(f32[2,256,7168]{2,1,0:T(8,128)} %param.7, f32[2,256]{1,0:T(2,128)} %param.8), kind=kLoop, calls=%fused_computation.16 | loop fusion | flops 3670016 | bytes 29362176 | tf_op jit(solution)/shard_map/mul | solution.py:62
  21.6 22.0 %copy.7 = f32[2,256,7168]{1,0,2:T(2,128)} copy(f32[2,256,7168]{2,1,0:T(8,128)} %broadcast_multiply_fusion) | data formatting | bytes 29360128 | tf_op jit(solution)/shard_map/mul | solution.py:62
  43.6 7.8 %gather_fusion.3 = f32[34,2,256,28]{2,1,3,0:T(2,128)S(1)} fusion(f32[2,256,256,28]{1,0,3,2:T(2,128)} %bitcast.83, s32[1024]{0:T(1024)S(1)} %pad_clamp_fusion.12), kind=kCustom, calls=%fused_computation.9.clone | custom fusion | bytes 3899528 | tf_op jit(solution)/shard_map/jit(_take)/gather | solution.py:70
  61.5 9.5 %gather_fusion.7 = f32[34,2,256,28]{2,1,3,0:T(2,128)} fusion(f32[2,256,256,28]{1,0,3,2:T(2,128)} %bitcast.84, s32[1024]{0:T(1024)S(1)} %pad_clamp_fusion.8), kind=kCustom, calls=%fused_computation.11.clone | custom fusion | bytes 3899528 | tf_op jit(solution)/shard_map/jit(_take)/gather | solution.py:70
  82.2 9.5 %gather_fusion.9 = f32[34,2,256,28]{2,1,3,0:T(2,128)} fusion(f32[2,256,256,28]{1,0,3,2:T(2,128)} %bitcast.85, s32[1024]{0:T(1024)S(1)} %pad_clamp_fusion.6), kind=kCustom, calls=%fused_computation.12.clone | custom fusion | bytes 3899528 | tf_op jit(solution)/shard_map/jit(_take)/gather | solution.py:70
  101.3 9.5 %gather_fusion.13 = f32[34,2,256,28]{2,1,3,0:T(2,128)} fusion(f32[2,256,256,28]{1,0,3,2:T(2,128)} %bitcast.86, s32[1024]{0:T(1024)S(1)} %pad_clamp_fusion.2), kind=kCustom, calls=%fused_computation.14.clone | custom fusion | bytes 3899528 | tf_op jit(solution)/shard_map/jit(_take)/gather | solution.py:70
  118.3 14.2 %collective-permute-start.5 = (f32[17,56,512]{2,1,0:T(8,128)}, f32[17,56,512]{2,1,0:T(8,128)}, u32[]{:S(2)}, u32[]{:S(2)}) collective-permute-start(f32[17,56,512]{2,1,0:T(8,128)} %reshape.71), channel_id=1, source_target_pairs={{0,12},{2,14},{4,0},{6,2},{8,4},{10,6},{12,8},{14,10},{1,13},{3,15... | collective-permute-start | bytes 5849096 | tf_op jit(solution)/shard_map/ppermute | solution.py:74
  133.4 9.5 %gather_fusion.15 = f32[34,2,256,28]{2,1,3,0:T(2,128)} fusion(f32[2,256,256,28]{1,0,3,2:T(2,128)} %bitcast.87, s32[1024]{0:T(1024)S(1)} %pad_clamp_fusion), kind=kCustom, calls=%fused_computation.15.clone | custom fusion | bytes 3899528 | tf_op jit(solution)/shard_map/jit(_take)/gather | solution.py:70
  152.7 9.5 %gather_fusion.1 = f32[34,2,256,28]{2,1,3,0:T(2,128)} fusion(f32[2,256,256,28]{1,0,3,2:T(2,128)} %bitcast.88, s32[1024]{0:T(1024)S(1)} %pad_clamp_fusion.14), kind=kCustom, calls=%fused_computation.1.clone | custom fusion | bytes 3899528 | tf_op jit(solution)/shard_map/jit(_take)/gather | solution.py:70
  163.0 9.5 %gather_fusion.11 = f32[34,2,256,28]{2,1,3,0:T(2,128)} fusion(f32[2,256,256,28]{1,0,3,2:T(2,128)} %bitcast.89, s32[1024]{0:T(1024)S(1)} %pad_clamp_fusion.4), kind=kCustom, calls=%fused_computation.13.clone | custom fusion | bytes 3899528 | tf_op jit(solution)/shard_map/jit(_take)/gather | solution.py:70
  173.4 9.5 %gather_fusion.5 = f32[34,2,256,28]{2,1,3,0:T(2,128)} fusion(f32[2,256,256,28]{1,0,3,2:T(2,128)} %bitcast.90, s32[1024]{0:T(1024)S(1)} %pad_clamp_fusion.10), kind=kCustom, calls=%fused_computation.10.clone | custom fusion | bytes 3899528 | tf_op jit(solution)/shard_map/jit(_take)/gather | solution.py:70
  219.6 29.0 %collective-permute-done.6 = f32[17,56,512]{2,1,0:T(8,128)} collective-permute-done((f32[17,56,512]{2,1,0:T(8,128)}, f32[17,56,512]{2,1,0:T(8,128)}, u32[]{:S(2)}, u32[]{:S(2)}) %collective-permute-start.6) | collective-permute-done | bytes 1949728 | tf_op jit(solution)/shard_map/ppermute | solution.py:74
  272.4 65.5 %collective-permute-done.4 = f32[17,56,512]{2,1,0:T(8,128)S(1)} collective-permute-done((f32[17,56,512]{2,1,0:T(8,128)S(1)}, f32[17,56,512]{2,1,0:T(8,128)S(1)}, u32[]{:S(2)}, u32[]{:S(2)}) %collective-permute-start.4) | collective-permute-done | bytes 1949728 | tf_op jit(solution)/shard_map/ppermute | solution.py:74
  357.8 23.3 %collective-permute-done.1 = f32[17,56,512]{2,1,0:T(8,128)S(1)} collective-permute-done((f32[17,56,512]{2,1,0:T(8,128)S(1)}, f32[17,56,512]{2,1,0:T(8,128)S(1)}, u32[]{:S(2)}, u32[]{:S(2)}) %collective-permute-start.1) | collective-permute-done | bytes 1949728 | tf_op jit(solution)/shard_map/ppermute | solution.py:74
  390.4 74.6 %all-reduce.2.cloned.1.call-done = f32[33,56,56]{2,1,0:T(8,128)} async-done(((f32[33,56,56]{2,1,0:T(8,128)}), f32[33,56,56]{2,1,0:T(8,128)}) %all-reduce.2.cloned.1.call-update) | async-done | bytes 413968 | tf_op jit(solution)/shard_map/psum | solution.py:79
  468.7 12.0 %shard_map.37 = f32[17,56,56]{2,1,0:T(8,128)} custom-call(f32[17,56,56]{2,1,0:T(8,128)} %fusion.118.sq_ref, f32[17,56,56]{2,1,0:T(8,128)} %slice.163.s_ref), custom_call_target="tpu_custom_call" | custom-call | tf_op jit(solution)/shard_map/pallas_call | solution.py:37
  491.9 11.7 %shard_map.38 = f32[16,56,56]{2,1,0:T(8,128)} custom-call(f32[16,56,56]{2,1,0:T(8,128)} %fusion.128.sq_ref, f32[16,56,56]{2,1,0:T(8,128)} %copy-done.22), custom_call_target="tpu_custom_call" | custom-call | tf_op jit(solution)/shard_map/pallas_call | solution.py:37
  513.6 4.4 fusion.60
  524.7 4.3 fusion.57
  545.0 4.4 fusion.51
  555.9 4.4 fusion.48
  581.1 4.3 convolution_add_fusion
  588.7 7.4 %broadcast_in_dim.19 = f32[32,28,2,2048]{3,2,1,0:T(2,128)S(1)} broadcast(f32[]{:T(128)} %constant.165.clone.1), dimensions={} | broadcast | bytes 14680068 | tf_op jit(solution)/shard_map/broadcast_in_dim | solution.py:99
  606.3 5.5 copy-done.12
  (179 shorter events, 230.8 us)
Async XLA Ops:
  6.5 458.4 %all-reduce.2.cloned.1.call-start = ((), (), s32[]{:S(2)}) async-start(), calls=%async_computation | async-start | bytes 1892352 | tf_op jit(solution)/shard_map/psum | solution.py:79
  57.4 325.4 %collective-permute-start = (f32[17,56,512]{2,1,0:T(8,128)}, f32[17,56,512]{2,1,0:T(8,128)S(1)}, u32[]{:S(2)}, u32[]{:S(2)}) collective-permute-start(f32[17,56,512]{2,1,0:T(8,128)} %reshape.66), channel_id=1, source_target_pairs={{0,2},{2,4},{4,6},{6,8},{8,10},{10,12},{12,14},{14,0},{1,3},{3,5},... | collective-permute-start | bytes 5849096 | tf_op jit(solution)/shard_map/ppermute | solution.py:74
  78.5 271.4 %collective-permute-start.2 = (f32[17,56,512]{2,1,0:T(8,128)}, f32[17,56,512]{2,1,0:T(8,128)}, u32[]{:S(2)}, u32[]{:S(2)}) collective-permute-start(f32[17,56,512]{2,1,0:T(8,128)} %reshape.68), channel_id=1, source_target_pairs={{0,6},{2,8},{4,10},{6,12},{8,14},{10,0},{12,2},{14,4},{1,7},{3,9},... | collective-permute-start | bytes 5849096 | tf_op jit(solution)/shard_map/ppermute | solution.py:74
  99.3 165.2 %collective-permute-start.3 = (f32[17,56,512]{2,1,0:T(8,128)}, f32[17,56,512]{2,1,0:T(8,128)}, u32[]{:S(2)}, u32[]{:S(2)}) collective-permute-start(f32[17,56,512]{2,1,0:T(8,128)} %reshape.69), channel_id=1, source_target_pairs={{0,8},{2,10},{4,12},{6,14},{8,0},{10,2},{12,4},{14,6},{1,9},{3,11}... | collective-permute-start | bytes 5849096 | tf_op jit(solution)/shard_map/ppermute | solution.py:74
  118.3 138.2 %collective-permute-start.5 = (f32[17,56,512]{2,1,0:T(8,128)}, f32[17,56,512]{2,1,0:T(8,128)}, u32[]{:S(2)}, u32[]{:S(2)}) collective-permute-start(f32[17,56,512]{2,1,0:T(8,128)} %reshape.71), channel_id=1, source_target_pairs={{0,12},{2,14},{4,0},{6,2},{8,4},{10,6},{12,8},{14,10},{1,13},{3,15... | collective-permute-start | bytes 5849096 | tf_op jit(solution)/shard_map/ppermute | solution.py:74
  150.5 98.1 %collective-permute-start.6 = (f32[17,56,512]{2,1,0:T(8,128)}, f32[17,56,512]{2,1,0:T(8,128)}, u32[]{:S(2)}, u32[]{:S(2)}) collective-permute-start(f32[17,56,512]{2,1,0:T(8,128)} %reshape.72), channel_id=1, source_target_pairs={{0,14},{2,0},{4,2},{6,4},{8,6},{10,8},{12,10},{14,12},{1,15},{3,1}... | collective-permute-start | bytes 5849096 | tf_op jit(solution)/shard_map/ppermute | solution.py:74
  185.5 3.0 copy-start.7
  196.1 3.9 copy-start.8
  196.1 3.9 copy-start.10
  215.4 33.2 %copy-start.25 = (f32[17,56,512]{2,1,0:T(8,128)S(1)}, f32[17,56,512]{2,1,0:T(8,128)}, u32[]{:S(2)}) copy-start(f32[17,56,512]{2,1,0:T(8,128)} %reshape.70) | copy-start | bytes 5849092
  219.5 37.0 %copy-start.24 = (f32[17,56,512]{2,1,0:T(8,128)S(1)}, f32[17,56,512]{2,1,0:T(8,128)}, u32[]{:S(2)}) copy-start(f32[17,56,512]{2,1,0:T(8,128)} %reshape.67) | copy-start | bytes 5849092
  248.6 89.3 %collective-permute-start.4 = (f32[17,56,512]{2,1,0:T(8,128)S(1)}, f32[17,56,512]{2,1,0:T(8,128)S(1)}, u32[]{:S(2)}, u32[]{:S(2)}) collective-permute-start(f32[17,56,512]{2,1,0:T(8,128)S(1)} %copy-done.25), channel_id=1, source_target_pairs={{0,10},{2,12},{4,14},{6,0},{8,2},{10,4},{12,6},{14,8},{1,11},{3,13... | collective-permute-start | bytes 5849096 | tf_op jit(solution)/shard_map/ppermute | solution.py:74
  256.6 124.6 %collective-permute-start.1 = (f32[17,56,512]{2,1,0:T(8,128)S(1)}, f32[17,56,512]{2,1,0:T(8,128)S(1)}, u32[]{:S(2)}, u32[]{:S(2)}) collective-permute-start(f32[17,56,512]{2,1,0:T(8,128)S(1)} %copy-done.24), channel_id=1, source_target_pairs={{0,4},{2,6},{4,8},{6,10},{8,12},{10,14},{12,0},{14,2},{1,5},{3,7},... | collective-permute-start | bytes 5849096 | tf_op jit(solution)/shard_map/ppermute | solution.py:74
  381.1 3.7 copy-start.2
  465.0 2.9 copy-start.23
  480.7 3.9 copy-start.13
  503.6 4.0 copy-start.11
  532.4 3.2 copy-start.5
  563.5 3.2 copy-start.3
  577.6 3.5 copy-start.9
  588.7 7.4 %copy-start.21 = (f32[32,28,2,256]{3,2,1,0:T(2,128)S(1)}, f32[32,28,2,256]{3,2,1,0:T(2,128)}, u32[]{:S(2)}) copy-start(f32[32,28,2,256]{3,2,1,0:T(2,128)} %reshape.73) | copy-start | bytes 5505028
  605.1 6.6 %copy-start.14 = (f32[32,28,2,256]{3,2,1,0:T(2,128)S(1)}, f32[32,28,2,256]{3,2,1,0:T(2,128)}, u32[]{:S(2)}) copy-start(f32[32,28,2,256]{3,2,1,0:T(2,128)} %reshape.80) | copy-start | bytes 5505028
  605.1 8.5 %copy-start.1 = (s32[256]{0:T(256)S(1)}, s32[256]{0:T(256)}, u32[]{:S(2)}) copy-start(s32[256]{0:T(256)} %param.9) | copy-start | bytes 3076
  606.3 5.5 copy-start.12
  (12 other events, 19.3 us)
Sparse Core Ops, SparseCore 0:
  390.0 74.9 all-reduce.1
